TPU v7x, 512 devices: a whole 4x4x16 slice. The times are simulated.
512 devices in a mesh: ctx: 64 (over x_hi, z, core), head: 8 (over x_lo, y).
Axes of the slice: x: 4 (x_hi: 2, x_lo: 2; x = x_hi * 2 + x_lo), y: 4, z: 16, core: 2. Of those that a mesh axis runs over, the one named last changes fastest.
Arguments:
- q_latent: bfloat16 [8192, 64, 512], P('ctx', 'head'), may hold values from -1.25 to 1.25
- q_rope: bfloat16 [8192, 4096], P('ctx', 'head'), may hold values from -1.25 to 1.25
- attn_out: bfloat16 [8192, 64, 512], P('ctx', 'head'), may hold values from -4 to 4
- grad_out: bfloat16 [8192, 64, 512], P('ctx', 'head'), may hold values from -1 to 1
- log_total: float32 [8192, 64], P('ctx', 'head'), may hold values from 4 to 6
- latent: bfloat16 [8192, 512], P('ctx'), may hold values from -2.5 to 2.5
- key_rope: bfloat16 [8192, 64], P('ctx'), may hold values from -2.5 to 2.5
- doc_start: int32 [8192], P('ctx'), may hold values from 0 to 8191, as said below
Outputs:
- grad_q_latent: bfloat16 [8192, 64, 512], P('ctx', 'head')
- grad_q_rope: bfloat16 [8192, 4096], P('ctx', 'head')
- grad_latent: bfloat16 [8192, 512], P(('ctx', 'head'))
- grad_key_rope: bfloat16 [8192, 64], P(('ctx', 'head'))
Inputs may be any that keep to these rules, and one draw needn't show every extreme that they name: doc_start[t] is the first token of the document that holds token t. Documents are runs of 1 to 897 tokens laid end to end from token 0; one document has exactly 897 tokens, and the last token of the sequence is a document of its own.
All inputs are finite; a program needn't handle non-finite values.
Results may differ from a plain program's by a relative error of at most 0.0056.
Values may be sent and summed in bfloat16 or wider, within the bound.
No kernel may reach another device: no remote copies, remote signals or barrier semaphores. Data moves between devices by JAX's collectives and lax.ppermute only.
A program may use at most 64 MiB of HBM per device.

v0:
```python
import jax
import jax.numpy as jnp
from jax import lax
from jax.sharding import PartitionSpec as P

ROPE = 64
NOPE = 128
LEVELS = 3


def shifted(x, axis, by):
    count = lax.axis_size(axis)
    pairs = [(i, i + by) for i in range(count) if 0 <= i + by < count]
    return lax.ppermute(x, axis, pairs)


def local(q_latent, q_rope, attn_out, grad_out, log_total, latent, key_rope, doc_start):
    tok_rows, head_count, lat_width = q_latent.shape
    rope_width = key_rope.shape[1]
    span = 2**LEVELS
    groups = lax.axis_size("head")
    softmax_scale = (NOPE + ROPE) ** (-0.5)
    q_rot = q_rope.reshape(tok_rows, head_count, rope_width)
    row_delta = jnp.einsum("thc,thc->th", grad_out, attn_out, preferred_element_type=jnp.float32)
    own_tile = lax.axis_index("ctx")
    query_pos = own_tile * tok_rows + jnp.arange(tok_rows, dtype=jnp.int32)
    keys = jnp.concatenate([latent, key_rope], axis=1)[None]
    width = 1
    while width < span:
        keys = jnp.concatenate([shifted(keys, "ctx", width), keys], axis=0)
        width *= 2
    keys = keys.reshape(span * tok_rows, lat_width + rope_width)
    lat_all = keys[:, :lat_width]
    rot_all = keys[:, lat_width:]
    key_pos = (own_tile - span + 1) * tok_rows + jnp.arange(span * tok_rows, dtype=jnp.int32)
    visible = ((key_pos[None, :] >= doc_start[:, None]) & (key_pos[None, :] <= query_pos[:, None]))[
        :, None, :
    ]
    scores = (
        jnp.einsum("thc,kc->thk", q_latent, lat_all, preferred_element_type=jnp.float32)
        + jnp.einsum("thr,kr->thk", q_rot, rot_all, preferred_element_type=jnp.float32)
    ) * softmax_scale
    probs = jnp.where(
        visible, jnp.exp(jnp.where(visible, scores, 0.0) - log_total[:, :, None]), 0.0
    )
    grad_probs = jnp.einsum("thc,kc->thk", grad_out, lat_all, preferred_element_type=jnp.float32)
    grad_scores = probs * (grad_probs - row_delta[:, :, None])
    probs_b = probs.astype(jnp.bfloat16)
    grad_b = grad_scores.astype(jnp.bfloat16)
    grad_qlat = softmax_scale * jnp.einsum(
        "thk,kc->thc", grad_b, lat_all, preferred_element_type=jnp.float32
    )
    grad_qrot = softmax_scale * jnp.einsum(
        "thk,kr->thr", grad_b, rot_all, preferred_element_type=jnp.float32
    )
    grad_lat = softmax_scale * jnp.einsum(
        "thk,thc->kc", grad_b, q_latent, preferred_element_type=jnp.float32
    ) + jnp.einsum("thk,thc->kc", probs_b, grad_out, preferred_element_type=jnp.float32)
    grad_rot = softmax_scale * jnp.einsum(
        "thk,thr->kr", grad_b, q_rot, preferred_element_type=jnp.float32
    )
    part = jnp.concatenate([grad_lat, grad_rot], axis=1)
    block = tok_rows // groups
    part = part.reshape(span, groups, block, lat_width + rope_width)
    part = lax.all_to_all(part, "head", 1, 1, tiled=True).sum(axis=1)
    width = span
    while width > 1:
        half = width // 2
        part = part[half:] + shifted(part[:half], "ctx", -half)
        width = half
    owned = part[0]
    return (
        grad_qlat.astype(jnp.bfloat16),
        grad_qrot.reshape(tok_rows, head_count * rope_width).astype(jnp.bfloat16),
        owned[:, :lat_width].astype(jnp.bfloat16),
        owned[:, lat_width:].astype(jnp.bfloat16),
    )


def solution(mesh):
    in_specs = (
        P("ctx", "head", None),
        P("ctx", "head"),
        P("ctx", "head", None),
        P("ctx", "head", None),
        P("ctx", "head"),
        P("ctx", None),
        P("ctx", None),
        P("ctx"),
    )
    out_specs = (
        P("ctx", "head", None),
        P("ctx", "head"),
        P(("ctx", "head"), None),
        P(("ctx", "head"), None),
    )
    return jax.shard_map(local, mesh=mesh, in_specs=in_specs, out_specs=out_specs, check_vma=False)
```

profile of v0, /device:TPU:69, one launch (start us, length us, event | category | flops | bytes accessed | tf_op | source)
XLA Modules:
  0.0 138.8 jit_solution(6973941782515152101)
XLA Ops:
  0.6 1.0 copy.44
  1.7 0.0 copy-start.1
  1.7 0.8 maximum_bitcast_fusion
  2.5 4.1 %collective-permute-start = (bf16[1,128,576]{1,2,0:T(8,128)(2,1)S(1)}, bf16[1,128,576]{1,2,0:T(8,128)(2,1)S(1)}, u32[]{:S(2)}, u32[]{:S(2)}) collective-permute-start(bf16[1,128,576]{1,2,0:T(8,128)(2,1)S(1)} %maximum_bitcast_fusion), channel_id=1, source_target_pairs={{0,8},{8,16},{16,24},{24,32},{32,40},{40,48},{48,56},{56,64},{64,7... | collective-permute-start | bytes 442376 | tf_op jit(solution)/shard_map/ppermute | solution.py:14
  6.6 2.1 %collective-permute-done = bf16[1,128,576]{1,2,0:T(8,128)(2,1)S(1)} collective-permute-done((bf16[1,128,576]{1,2,0:T(8,128)(2,1)S(1)}, bf16[1,128,576]{1,2,0:T(8,128)(2,1)S(1)}, u32[]{:S(2)}, u32[]{:S(2)}) %collective-permute-start) | collective-permute-done | bytes 147488 | tf_op jit(solution)/shard_map/ppermute | solution.py:14
  8.7 4.8 %collective-permute-start.1 = (bf16[2,128,576]{1,2,0:T(8,128)(2,1)S(1)}, bf16[2,128,576]{1,2,0:T(8,128)(2,1)S(1)}, u32[]{:S(2)}, u32[]{:S(2)}) collective-permute-start(bf16[2,128,576]{1,2,0:T(8,128)(2,1)S(1)} %pad_maximum_fusion.3), channel_id=1, source_target_pairs={{0,16},{8,24},{16,32},{24,40},{32,48},{40,56},{48,64},{56,72},{64,... | collective-permute-start | bytes 884744 | tf_op jit(solution)/shard_map/ppermute | solution.py:14
  13.5 1.9 %copy.56 = bf16[128,8,512]{0,2,1:T(8,128)(2,1)S(1)} copy(bf16[128,8,512]{2,1,0:T(8,128)(2,1)} %param.11) | data formatting | bytes 2097152 | tf_op args[3]
  15.5 0.0 copy-start.9
  15.5 4.6 %collective-permute-done.1 = bf16[2,128,576]{1,2,0:T(8,128)(2,1)S(1)} collective-permute-done((bf16[2,128,576]{1,2,0:T(8,128)(2,1)S(1)}, bf16[2,128,576]{1,2,0:T(8,128)(2,1)S(1)}, u32[]{:S(2)}, u32[]{:S(2)}) %collective-permute-start.1) | collective-permute-done | bytes 294944 | tf_op jit(solution)/shard_map/ppermute | solution.py:14
  20.1 0.1 pad_maximum_fusion.2
  20.2 0.0 copy-start.11
  20.2 4.4 %collective-permute-start.2 = (bf16[4,128,576]{1,2,0:T(8,128)(2,1)S(1)}, bf16[4,128,576]{1,2,0:T(8,128)(2,1)}, u32[]{:S(2)}, u32[]{:S(2)}) collective-permute-start(bf16[4,128,576]{1,2,0:T(8,128)(2,1)S(1)} %pad_maximum_fusion.2), channel_id=1, source_target_pairs={{0,32},{8,40},{16,48},{24,56},{32,64},{40,72},{48,80},{56,88},{64,... | collective-permute-start | bytes 1769480 | tf_op jit(solution)/shard_map/ppermute | solution.py:14
  24.6 1.6 %fusion.4 = f32[128,8]{1,0:T(8,128)S(1)} fusion(bf16[128,8,512]{2,1,0:T(8,128)(2,1)S(1)} %copy-done.1, bf16[128,8,512]{2,1,0:T(8,128)(2,1)} %param.10), kind=kLoop, calls=%fused_computation.10 | loop fusion | flops 2096128 | bytes 2101248
  26.2 0.8 copy.47
  27.0 2.7 %copy.54 = bf16[128,8,512]{0,2,1:T(8,128)(2,1)} copy(bf16[128,8,512]{2,1,0:T(8,128)(2,1)} %param.8) | data formatting | bytes 2097152 | tf_op args[0]
  29.7 0.8 compare_and_fusion
  30.5 4.9 %collective-permute-done.2 = bf16[4,128,576]{1,2,0:T(8,128)(2,1)} collective-permute-done((bf16[4,128,576]{1,2,0:T(8,128)(2,1)S(1)}, bf16[4,128,576]{1,2,0:T(8,128)(2,1)}, u32[]{:S(2)}, u32[]{:S(2)}) %collective-permute-start.2) | collective-permute-done | bytes 589856 | tf_op jit(solution)/shard_map/ppermute | solution.py:14
  35.4 1.3 pad_maximum_fusion.1
  36.7 0.7 copy.45
  37.4 0.0 copy-start.6
  37.5 1.7 %fusion.9 = f32[1024,128,8]{1,0,2:T(8,128)S(1)} fusion(bf16[128,8,64]{0,2,1:T(8,128)(2,1)} %bitcast.56, bf16[1024,576]{1,0:T(8,128)(2,1)S(1)} %bitcast.51), kind=kOutput, calls=%fused_computation.24 | convolution fusion | flops 134217728 | bytes 4587520 | tf_op jit(solution)/shard_map/thr,kr->thk/dot_general | solution.py:41
  39.2 1.7 %fusion.3 = f32[128,8,1024]{0,2,1:T(8,128)S(1)} fusion(f32[1024,128,8]{1,0,2:T(8,128)S(1)} %fusion.9, bf16[128,8,512]{0,2,1:T(8,128)(2,1)S(1)} %copy-done.6, f32[128,8]{0,1:T(8,128)S(1)} %copy-done.12, pred[128,1024]{0,1:T(8,128)(4,1)S(1)} %copy-done.10, bf16[1024,576]{1,0:T(8,128)(2,1)S(1)} %bitcast.52), kind=kOutput, calls=%fused_computation.5 | convolution fusion | flops 1078984704 | bytes 10620928 | tf_op jit(solution)/shard_map/thc,kc->thk/dot_general | solution.py:40
  40.9 1.3 fusion.5
  42.2 0.0 copy-start.5
  42.2 2.6 %fusion = bf16[128,8,1024]{0,2,1:T(8,128)(2,1)S(1)} fusion(f32[128,8,1024]{0,2,1:T(8,128)S(1)} %fusion.3, bf16[128,8,512]{0,2,1:T(8,128)(2,1)} %copy-done, f32[128,8]{0,1:T(8,128)S(1)} %copy.67, bf16[1024,576]{1,0:T(8,128)(2,1)S(1)} %bitcast.53), kind=kOutput, calls=%fused_computation.1 | convolution fusion | flops 1076887552 | bytes 8392704 | tf_op jit(solution)/shard_map/thc,kc->thk/dot_general | solution.py:46
  44.8 0.8 fusion.7
  45.6 1.3 bitcast_add_fusion
  46.9 1.6 %pad_maximum_fusion = f32[1024,576]{0,1:T(8,128)} fusion(f32[1024,64]{0,1:T(8,128)S(1)} %fusion.7, f32[1024,512]{0,1:T(8,128)S(1)} %bitcast_add_fusion), kind=kLoop, calls=%fused_computation.6 | loop fusion | flops 589824 | bytes 4718592 | tf_op jit(solution)/shard_map/concatenate | solution.py:62
  48.5 3.2 %copy.58 = f32[1024,576]{1,0:T(8,128)} copy(f32[1024,576]{0,1:T(8,128)} %pad_maximum_fusion) | data formatting | bytes 4718592 | tf_op jit(solution)/shard_map/concatenate | solution.py:62
  51.7 2.0 %copy.59 = f32[8,8,16,576]{3,2,0,1:T(8,128)S(1)} copy(f32[8,8,16,576]{3,2,1,0:T(8,128)} %bitcast.50) | data formatting | bytes 4718592 | tf_op jit(solution)/shard_map/reshape | solution.py:64
  53.6 32.7 %all_to_all.5 = f32[8,8,16,576]{3,2,0,1:T(8,128)} all-to-all(f32[8,8,16,576]{3,2,0,1:T(8,128)S(1)} %copy.59), channel_id=1, replica_groups=mesh['ctx'=64,'head'=8] {'head'}, dimensions={1} | all-to-all | bytes 4718592 | tf_op jit(solution)/shard_map/all_to_all | solution.py:65
  86.3 2.6 %reduce_sum.9 = f32[8,16,576]{2,1,0:T(8,128)} reduce(f32[8,8,16,576]{3,2,0,1:T(8,128)} %all_to_all.5, f32[]{:T(128)} %constant.4.clone.1), dimensions={1}, to_apply=%region_0.1 | reduce | flops 516096 | bytes 2654212 | tf_op jit(solution)/shard_map/reduce_sum | solution.py:65
  89.0 0.9 slice.45
  89.9 1.9 %collective-permute-start.3 = (f32[4,16,576]{2,1,0:T(8,128)S(1)}, f32[4,16,576]{2,1,0:T(8,128)S(1)}, u32[]{:S(2)}, u32[]{:S(2)}) collective-permute-start(f32[4,16,576]{2,1,0:T(8,128)S(1)} %slice.45), channel_id=1, source_target_pairs={{32,0},{40,8},{48,16},{56,24},{64,32},{72,40},{80,48},{88,56},{96,... | collective-permute-start | bytes 442376 | tf_op jit(solution)/shard_map/ppermute | solution.py:14
  91.8 23.1 %collective-permute-done.3 = f32[4,16,576]{2,1,0:T(8,128)S(1)} collective-permute-done((f32[4,16,576]{2,1,0:T(8,128)S(1)}, f32[4,16,576]{2,1,0:T(8,128)S(1)}, u32[]{:S(2)}, u32[]{:S(2)}) %collective-permute-start.3) | collective-permute-done | bytes 147488 | tf_op jit(solution)/shard_map/ppermute | solution.py:14
  115.0 0.9 slice_add_fusion
  115.9 7.0 %collective-permute-start.4 = (f32[2,16,576]{2,1,0:T(8,128)S(1)}, f32[2,16,576]{2,1,0:T(8,128)S(1)}, u32[]{:S(2)}, u32[]{:S(2)}) collective-permute-start(f32[2,16,576]{2,1,0:T(8,128)S(1)} %slice.47), channel_id=1, source_target_pairs={{16,0},{24,8},{32,16},{40,24},{48,32},{56,40},{64,48},{72,56},{80,... | collective-permute-start | bytes 221192 | tf_op jit(solution)/shard_map/ppermute | solution.py:14
  122.9 1.3 multiply_convert_fusion
  124.2 2.7 %collective-permute-done.4 = f32[2,16,576]{2,1,0:T(8,128)S(1)} collective-permute-done((f32[2,16,576]{2,1,0:T(8,128)S(1)}, f32[2,16,576]{2,1,0:T(8,128)S(1)}, u32[]{:S(2)}, u32[]{:S(2)}) %collective-permute-start.4) | collective-permute-done | bytes 73760 | tf_op jit(solution)/shard_map/ppermute | solution.py:14
  126.9 0.6 slice.49
  127.5 4.5 %collective-permute-start.5 = (f32[1,16,576]{2,1,0:T(8,128)}, f32[1,16,576]{2,1,0:T(8,128)}, u32[]{:S(2)}, u32[]{:S(2)}) collective-permute-start(f32[1,16,576]{2,1,0:T(8,128)} %slice.49), channel_id=1, source_target_pairs={{8,0},{16,8},{24,16},{32,24},{40,32},{48,40},{56,48},{64,56},{72,6... | collective-permute-start | bytes 110600 | tf_op jit(solution)/shard_map/ppermute | solution.py:14
  132.0 0.5 fusion.8
  132.6 1.5 %copy.60 = bf16[128,8,512]{2,1,0:T(8,128)(2,1)} copy(bf16[128,8,512]{2,0,1:T(8,128)(2,1)S(1)} %multiply_convert_fusion) | data formatting | bytes 2097152
  134.1 0.8 copy.61
  134.9 2.0 %collective-permute-done.5 = f32[1,16,576]{2,1,0:T(8,128)} collective-permute-done((f32[1,16,576]{2,1,0:T(8,128)}, f32[1,16,576]{2,1,0:T(8,128)}, u32[]{:S(2)}, u32[]{:S(2)}) %collective-permute-start.5) | collective-permute-done | bytes 36896 | tf_op jit(solution)/shard_map/ppermute | solution.py:14
  136.9 0.8 fusion.11
  137.6 0.6 slice.51
  138.2 0.6 slice.50
  (27 shorter events, 0.1 us)
Async XLA Ops:
  1.7 22.9 %copy-start.1 = (bf16[128,8,512]{2,1,0:T(8,128)(2,1)S(1)}, bf16[128,8,512]{2,1,0:T(8,128)(2,1)}, u32[]{:S(2)}) copy-start(bf16[128,8,512]{2,1,0:T(8,128)(2,1)} %param.11) | copy-start | bytes 3145732
  2.5 6.2 %collective-permute-start = (bf16[1,128,576]{1,2,0:T(8,128)(2,1)S(1)}, bf16[1,128,576]{1,2,0:T(8,128)(2,1)S(1)}, u32[]{:S(2)}, u32[]{:S(2)}) collective-permute-start(bf16[1,128,576]{1,2,0:T(8,128)(2,1)S(1)} %maximum_bitcast_fusion), channel_id=1, source_target_pairs={{0,8},{8,16},{16,24},{24,32},{32,40},{40,48},{48,56},{56,64},{64,7... | collective-permute-start | bytes 442376 | tf_op jit(solution)/shard_map/ppermute | solution.py:14
  8.7 17.5 %copy-start.2 = (bf16[1,128,576]{1,2,0:T(8,128)(2,1)}, bf16[1,128,576]{1,2,0:T(8,128)(2,1)S(1)}, u32[]{:S(2)}) copy-start(bf16[1,128,576]{1,2,0:T(8,128)(2,1)S(1)} %collective-permute-done) | copy-start | bytes 442372
  8.7 11.4 %collective-permute-start.1 = (bf16[2,128,576]{1,2,0:T(8,128)(2,1)S(1)}, bf16[2,128,576]{1,2,0:T(8,128)(2,1)S(1)}, u32[]{:S(2)}, u32[]{:S(2)}) collective-permute-start(bf16[2,128,576]{1,2,0:T(8,128)(2,1)S(1)} %pad_maximum_fusion.3), channel_id=1, source_target_pairs={{0,16},{8,24},{16,32},{24,40},{32,48},{40,56},{48,64},{56,72},{64,... | collective-permute-start | bytes 884744 | tf_op jit(solution)/shard_map/ppermute | solution.py:14
  15.4 25.5 %copy-start = (bf16[128,8,512]{0,2,1:T(8,128)(2,1)}, bf16[128,8,512]{0,2,1:T(8,128)(2,1)S(1)}, u32[]{:S(2)}) copy-start(bf16[128,8,512]{0,2,1:T(8,128)(2,1)S(1)} %copy.56) | copy-start | bytes 3145732
  15.5 10.8 %copy-start.9 = (bf16[128,512]{1,0:T(8,128)(2,1)S(1)}, bf16[128,512]{1,0:T(8,128)(2,1)}, u32[]{:S(2)}) copy-start(bf16[128,512]{1,0:T(8,128)(2,1)} %param.9) | copy-start | bytes 393220
  20.1 9.6 %copy-start.4 = (bf16[2,128,576]{1,2,0:T(8,128)(2,1)}, bf16[2,128,576]{1,2,0:T(8,128)(2,1)S(1)}, u32[]{:S(2)}) copy-start(bf16[2,128,576]{1,2,0:T(8,128)(2,1)S(1)} %collective-permute-done.1) | copy-start | bytes 884740
  20.2 9.5 %copy-start.11 = (s32[128]{0:T(128)S(1)}, s32[128]{0:T(128)}, u32[]{:S(2)}) copy-start(s32[128]{0:T(128)} %param.15) | copy-start | bytes 1540
  20.2 15.2 %collective-permute-start.2 = (bf16[4,128,576]{1,2,0:T(8,128)(2,1)S(1)}, bf16[4,128,576]{1,2,0:T(8,128)(2,1)}, u32[]{:S(2)}, u32[]{:S(2)}) collective-permute-start(bf16[4,128,576]{1,2,0:T(8,128)(2,1)S(1)} %pad_maximum_fusion.2), channel_id=1, source_target_pairs={{0,32},{8,40},{16,48},{24,56},{32,64},{40,72},{48,80},{56,88},{64,... | collective-permute-start | bytes 1769480 | tf_op jit(solution)/shard_map/ppermute | solution.py:14
  26.2 9.2 %copy-start.3 = (bf16[1,128,576]{1,2,0:T(8,128)(2,1)S(1)}, bf16[1,128,576]{1,2,0:T(8,128)(2,1)}, u32[]{:S(2)}) copy-start(bf16[1,128,576]{1,2,0:T(8,128)(2,1)} %copy-done.2) | copy-start | bytes 442372
  37.4 1.7 %copy-start.6 = (bf16[128,8,512]{0,2,1:T(8,128)(2,1)S(1)}, bf16[128,8,512]{0,2,1:T(8,128)(2,1)}, u32[]{:S(2)}) copy-start(bf16[128,8,512]{0,2,1:T(8,128)(2,1)} %copy.54) | copy-start | bytes 3145732
  37.5 1.7 %copy-start.10 = (pred[128,1024]{0,1:T(8,128)(4,1)S(1)}, pred[128,1024]{0,1:T(8,128)(4,1)}, u32[]{:S(2)}) copy-start(pred[128,1024]{0,1:T(8,128)(4,1)} %compare_and_fusion) | copy-start | bytes 393220
  37.5 1.7 %copy-start.12 = (f32[128,8]{0,1:T(8,128)S(1)}, f32[128,8]{0,1:T(8,128)}, u32[]{:S(2)}) copy-start(f32[128,8]{0,1:T(8,128)} %param.12) | copy-start | bytes 12292
  42.2 2.6 %copy-start.5 = (bf16[128,512]{0,1:T(8,128)(2,1)S(1)}, bf16[128,512]{0,1:T(8,128)(2,1)}, u32[]{:S(2)}) copy-start(bf16[128,512]{0,1:T(8,128)(2,1)} %copy.47) | copy-start | bytes 393220
  89.9 25.1 %collective-permute-start.3 = (f32[4,16,576]{2,1,0:T(8,128)S(1)}, f32[4,16,576]{2,1,0:T(8,128)S(1)}, u32[]{:S(2)}, u32[]{:S(2)}) collective-permute-start(f32[4,16,576]{2,1,0:T(8,128)S(1)} %slice.45), channel_id=1, source_target_pairs={{32,0},{40,8},{48,16},{56,24},{64,32},{72,40},{80,48},{88,56},{96,... | collective-permute-start | bytes 442376 | tf_op jit(solution)/shard_map/ppermute | solution.py:14
  115.9 11.0 %collective-permute-start.4 = (f32[2,16,576]{2,1,0:T(8,128)S(1)}, f32[2,16,576]{2,1,0:T(8,128)S(1)}, u32[]{:S(2)}, u32[]{:S(2)}) collective-permute-start(f32[2,16,576]{2,1,0:T(8,128)S(1)} %slice.47), channel_id=1, source_target_pairs={{16,0},{24,8},{32,16},{40,24},{48,32},{56,40},{64,48},{72,56},{80,... | collective-permute-start | bytes 221192 | tf_op jit(solution)/shard_map/ppermute | solution.py:14
  126.9 0.6 copy-start.7
  127.5 9.3 %collective-permute-start.5 = (f32[1,16,576]{2,1,0:T(8,128)}, f32[1,16,576]{2,1,0:T(8,128)}, u32[]{:S(2)}, u32[]{:S(2)}) collective-permute-start(f32[1,16,576]{2,1,0:T(8,128)} %slice.49), channel_id=1, source_target_pairs={{8,0},{16,8},{24,16},{32,24},{40,32},{48,40},{56,48},{64,56},{72,6... | collective-permute-start | bytes 110600 | tf_op jit(solution)/shard_map/ppermute | solution.py:14
  132.6 4.3 %copy-start.8 = (f32[2,16,576]{2,1,0:T(8,128)S(1)}, f32[2,16,576]{2,1,0:T(8,128)}, u32[]{:S(2)}) copy-start(f32[2,16,576]{2,1,0:T(8,128)} %copy-done.7) | copy-start | bytes 221188
where the time goes:
time: 140 us; the launch traced here: 139 us
  waiting for transfers between devices  39.3 us (28%)
  blocking collectives  32.7 us (23%)
  starting transfers between devices  26.7 us (19%)
  local copies, waits for them, and re-layouts  17.5 us (12%)
  matrix products  11.1 us (8%)
  other arithmetic  10.7 us (8%)
    ppermute x6, waiting for transfers between devices, shifted(): return lax.ppermute(x, axis, pairs)  39.3 us
    all_to_all x1, blocking collectives, local(): part = lax.all_to_all(part, 'head', 1, 1, tiled=True).sum(axis=1)  32.7 us
    ppermute x6, starting transfers between devices, shifted(): return lax.ppermute(x, axis, pairs)  26.7 us
    unnamed x32, local copies, waits for them, and re-layouts  8.78 us
    concatenate x1, local copies, waits for them, and re-layouts, local(): part = jnp.concatenate([grad_lat, grad_rot], axis=1)  3.18 us
  transfers between devices with their start and end apart: 6, of which 6 were waited for; matrix products, arithmetic and copies ran while one was open for 9% of the time, Pallas kernels for 0%

commit v1 on v0

--- a/solution.py
+++ b/solution.py
@@ -62,7 +62,10 @@
     part = jnp.concatenate([grad_lat, grad_rot], axis=1)
     block = tok_rows // groups
     part = part.reshape(span, groups, block, lat_width + rope_width)
-    part = lax.all_to_all(part, "head", 1, 1, tiled=True).sum(axis=1)
+    part = jnp.concatenate(
+        lax.all_to_all(jnp.stack(jnp.split(part, lax.axis_size("head"), axis=1)), "head", 0, 0),
+        axis=1,
+    ).sum(axis=1)
     width = span
     while width > 1:
         half = width // 2

time: 140 us -> 142 us (1.014)
  local copies, waits for them, and re-layouts: 17.5 us -> 19.9 us
    unnamed x32 -> x37, local copies, waits for them, and re-layouts: 8.78 us -> 13.1 us
    reshape x1 -> x0, local copies, waits for them, and re-layouts: 1.98 us -> none  [local(): part = part.reshape(span, groups, block, lat_width + rope_width)]
where the time goes in v1:
time: 142 us; the launch traced here: 141 us
  waiting for transfers between devices  39.3 us (28%)
  blocking collectives  32.7 us (23%)
  starting transfers between devices  26.5 us (19%)
  local copies, waits for them, and re-layouts  19.9 us (14%)
  matrix products  11.1 us (8%)
  other arithmetic  10.7 us (8%)
    ppermute x6, waiting for transfers between devices, shifted(): return lax.ppermute(x, axis, pairs)  39.3 us
    all_to_all x1, blocking collectives, local(): lax.all_to_all(jnp.stack(jnp.split(part, lax.axis_size('head'), axis=1)),...  32.7 us
    ppermute x6, starting transfers between devices, shifted(): return lax.ppermute(x, axis, pairs)  26.5 us
    unnamed x37, local copies, waits for them, and re-layouts  13.1 us
    concatenate x1, local copies, waits for them, and re-layouts, local(): part = jnp.concatenate([grad_lat, grad_rot], axis=1)  3.19 us
  transfers between devices with their start and end apart: 6, of which 6 were waited for; matrix products, arithmetic and copies ran while one was open for 9% of the time, Pallas kernels for 0%

profile of v1, /device:TPU:69, one launch (start us, length us, event | category | flops | bytes accessed | tf_op | source)
XLA Modules:
  0.0 141.1 jit_solution(17706311028627163974)
XLA Ops:
  0.6 0.0 copy-start.2
  0.6 1.1 copy.58
  1.8 0.7 maximum_bitcast_fusion
  2.5 4.1 %collective-permute-start = (bf16[1,128,576]{1,2,0:T(8,128)(2,1)S(1)}, bf16[1,128,576]{1,2,0:T(8,128)(2,1)S(1)}, u32[]{:S(2)}, u32[]{:S(2)}) collective-permute-start(bf16[1,128,576]{1,2,0:T(8,128)(2,1)S(1)} %maximum_bitcast_fusion), channel_id=1, source_target_pairs={{0,8},{8,16},{16,24},{24,32},{32,40},{40,48},{48,56},{56,64},{64,7... | collective-permute-start | bytes 442376 | tf_op jit(solution)/shard_map/ppermute | solution.py:14
  6.6 2.1 %collective-permute-done = bf16[1,128,576]{1,2,0:T(8,128)(2,1)S(1)} collective-permute-done((bf16[1,128,576]{1,2,0:T(8,128)(2,1)S(1)}, bf16[1,128,576]{1,2,0:T(8,128)(2,1)S(1)}, u32[]{:S(2)}, u32[]{:S(2)}) %collective-permute-start) | collective-permute-done | bytes 147488 | tf_op jit(solution)/shard_map/ppermute | solution.py:14
  8.7 4.8 %collective-permute-start.1 = (bf16[2,128,576]{1,2,0:T(8,128)(2,1)S(1)}, bf16[2,128,576]{1,2,0:T(8,128)(2,1)S(1)}, u32[]{:S(2)}, u32[]{:S(2)}) collective-permute-start(bf16[2,128,576]{1,2,0:T(8,128)(2,1)S(1)} %pad_maximum_fusion.3), channel_id=1, source_target_pairs={{0,16},{8,24},{16,32},{24,40},{32,48},{40,56},{48,64},{56,72},{64,... | collective-permute-start | bytes 884744 | tf_op jit(solution)/shard_map/ppermute | solution.py:14
  13.5 2.0 %copy.70 = bf16[128,8,512]{0,2,1:T(8,128)(2,1)S(1)} copy(bf16[128,8,512]{2,1,0:T(8,128)(2,1)} %param.11) | data formatting | bytes 2097152 | tf_op args[3]
  15.5 4.6 %collective-permute-done.1 = bf16[2,128,576]{1,2,0:T(8,128)(2,1)S(1)} collective-permute-done((bf16[2,128,576]{1,2,0:T(8,128)(2,1)S(1)}, bf16[2,128,576]{1,2,0:T(8,128)(2,1)S(1)}, u32[]{:S(2)}, u32[]{:S(2)}) %collective-permute-start.1) | collective-permute-done | bytes 294944 | tf_op jit(solution)/shard_map/ppermute | solution.py:14
  20.1 0.1 pad_maximum_fusion.2
  20.2 4.3 %collective-permute-start.2 = (bf16[4,128,576]{1,2,0:T(8,128)(2,1)S(1)}, bf16[4,128,576]{1,2,0:T(8,128)(2,1)}, u32[]{:S(2)}, u32[]{:S(2)}) collective-permute-start(bf16[4,128,576]{1,2,0:T(8,128)(2,1)S(1)} %pad_maximum_fusion.2), channel_id=1, source_target_pairs={{0,32},{8,40},{16,48},{24,56},{32,64},{40,72},{48,80},{56,88},{64,... | collective-permute-start | bytes 1769480 | tf_op jit(solution)/shard_map/ppermute | solution.py:14
  24.4 1.6 %fusion.4 = f32[128,8]{1,0:T(8,128)S(1)} fusion(bf16[128,8,512]{2,1,0:T(8,128)(2,1)S(1)} %copy-done.2, bf16[128,8,512]{2,1,0:T(8,128)(2,1)} %param.10), kind=kLoop, calls=%fused_computation.10 | loop fusion | flops 2096128 | bytes 2101248
  26.1 0.8 copy.61
  26.9 2.7 %copy.68 = bf16[128,8,512]{0,2,1:T(8,128)(2,1)} copy(bf16[128,8,512]{2,1,0:T(8,128)(2,1)} %param.8) | data formatting | bytes 2097152 | tf_op args[0]
  29.5 0.9 compare_and_fusion
  30.4 5.0 %collective-permute-done.2 = bf16[4,128,576]{1,2,0:T(8,128)(2,1)} collective-permute-done((bf16[4,128,576]{1,2,0:T(8,128)(2,1)S(1)}, bf16[4,128,576]{1,2,0:T(8,128)(2,1)}, u32[]{:S(2)}, u32[]{:S(2)}) %collective-permute-start.2) | collective-permute-done | bytes 589856 | tf_op jit(solution)/shard_map/ppermute | solution.py:14
  35.4 1.4 %pad_maximum_fusion.1 = bf16[8,128,576]{1,2,0:T(8,128)(2,1)S(1)} fusion(bf16[1,128,576]{1,2,0:T(8,128)(2,1)S(1)} %maximum_bitcast_fusion, bf16[1,128,576]{1,2,0:T(8,128)(2,1)} %copy-done.3, bf16[2,128,576]{1,2,0:T(8,128)(2,1)} %copy-done.4, bf16[4,128,576]{1,2,0:T(8,128)(2,1)} %collective-permute-done.2), kind=kLoop, calls=%fused_computation.14 | loop fusion | flops 1769472 | bytes 2359296 | tf_op jit(solution)/shard_map/concatenate | solution.py:30
  36.8 0.7 copy.59
  37.6 0.0 copy-start.11
  37.6 1.7 %fusion.17 = f32[1024,128,8]{1,0,2:T(8,128)S(1)} fusion(bf16[128,8,64]{0,2,1:T(8,128)(2,1)} %bitcast.109, bf16[1024,576]{1,0:T(8,128)(2,1)S(1)} %bitcast.104), kind=kOutput, calls=%fused_computation.40 | convolution fusion | flops 134217728 | bytes 4587520 | tf_op jit(solution)/shard_map/thr,kr->thk/dot_general | solution.py:41
  39.3 1.7 %fusion.3 = f32[128,8,1024]{0,2,1:T(8,128)S(1)} fusion(f32[1024,128,8]{1,0,2:T(8,128)S(1)} %fusion.17, bf16[128,8,512]{0,2,1:T(8,128)(2,1)S(1)} %copy-done.6, f32[128,8]{0,1:T(8,128)S(1)} %copy-done.11, pred[128,1024]{0,1:T(8,128)(4,1)S(1)} %copy-done.9, bf16[1024,576]{1,0:T(8,128)(2,1)S(1)} %bitcast.105), kind=kOutput, calls=%fused_computation.5 | convolution fusion | flops 1078984704 | bytes 10620928 | tf_op jit(solution)/shard_map/thc,kc->thk/dot_general | solution.py:40
  41.0 1.3 fusion.5
  42.3 2.6 %fusion = bf16[128,8,1024]{0,2,1:T(8,128)(2,1)S(1)} fusion(f32[128,8,1024]{0,2,1:T(8,128)S(1)} %fusion.3, bf16[128,8,512]{0,2,1:T(8,128)(2,1)} %copy-done.1, f32[128,8]{0,1:T(8,128)S(1)} %copy.87, bf16[1024,576]{1,0:T(8,128)(2,1)S(1)} %bitcast.106), kind=kOutput, calls=%fused_computation.1 | convolution fusion | flops 1076887552 | bytes 8392704 | tf_op jit(solution)/shard_map/thc,kc->thk/dot_general | solution.py:46
  44.9 0.8 fusion.7
  45.7 1.3 bitcast_add_fusion
  47.0 1.6 %pad_maximum_fusion = f32[1024,576]{0,1:T(8,128)} fusion(f32[1024,64]{0,1:T(8,128)S(1)} %fusion.7, f32[1024,512]{0,1:T(8,128)S(1)} %bitcast_add_fusion), kind=kLoop, calls=%fused_computation.6 | loop fusion | flops 589824 | bytes 4718592 | tf_op jit(solution)/shard_map/concatenate | solution.py:62
  48.6 3.2 %copy.72 = f32[1024,576]{1,0:T(8,128)} copy(f32[1024,576]{0,1:T(8,128)} %pad_maximum_fusion) | data formatting | bytes 4718592 | tf_op jit(solution)/shard_map/concatenate | solution.py:62
  51.8 1.1 fusion.16
  52.9 1.0 fusion.15
  53.9 1.0 fusion.14
  54.9 1.0 fusion.13
  56.1 32.7 %all_to_all.5 = f32[8,8,1,16,576]{4,3,1,2,0:T(8,128)} all-to-all(f32[8,8,1,16,576]{4,3,1,2,0:T(8,128)S(1)} %fusion.9), channel_id=1, replica_groups=mesh['ctx'=64,'head'=8] {'head'}, dimensions={0} | all-to-all | bytes 4718592 | tf_op jit(solution)/shard_map/all_to_all | solution.py:66
  88.7 2.6 %reduce_sum.9 = f32[8,16,576]{2,1,0:T(8,128)} reduce(f32[8,8,1,16,576]{4,3,1,2,0:T(8,128)} %all_to_all.5, f32[]{:T(128)} %constant.4.clone.1), dimensions={0,2}, to_apply=%region_0.1 | reduce | flops 516096 | bytes 2654212 | tf_op jit(solution)/shard_map/reduce_sum | solution.py:68
  91.4 0.9 slice.45
  92.3 1.9 %collective-permute-start.3 = (f32[4,16,576]{2,1,0:T(8,128)S(1)}, f32[4,16,576]{2,1,0:T(8,128)S(1)}, u32[]{:S(2)}, u32[]{:S(2)}) collective-permute-start(f32[4,16,576]{2,1,0:T(8,128)S(1)} %slice.45), channel_id=1, source_target_pairs={{32,0},{40,8},{48,16},{56,24},{64,32},{72,40},{80,48},{88,56},{96,... | collective-permute-start | bytes 442376 | tf_op jit(solution)/shard_map/ppermute | solution.py:14
  94.2 23.0 %collective-permute-done.3 = f32[4,16,576]{2,1,0:T(8,128)S(1)} collective-permute-done((f32[4,16,576]{2,1,0:T(8,128)S(1)}, f32[4,16,576]{2,1,0:T(8,128)S(1)}, u32[]{:S(2)}, u32[]{:S(2)}) %collective-permute-start.3) | collective-permute-done | bytes 147488 | tf_op jit(solution)/shard_map/ppermute | solution.py:14
  117.2 0.9 slice_add_fusion
  118.2 7.0 %collective-permute-start.4 = (f32[2,16,576]{2,1,0:T(8,128)S(1)}, f32[2,16,576]{2,1,0:T(8,128)S(1)}, u32[]{:S(2)}, u32[]{:S(2)}) collective-permute-start(f32[2,16,576]{2,1,0:T(8,128)S(1)} %slice.47), channel_id=1, source_target_pairs={{16,0},{24,8},{32,16},{40,24},{48,32},{56,40},{64,48},{72,56},{80,... | collective-permute-start | bytes 221192 | tf_op jit(solution)/shard_map/ppermute | solution.py:14
  125.2 1.3 multiply_convert_fusion
  126.5 2.7 %collective-permute-done.4 = f32[2,16,576]{2,1,0:T(8,128)S(1)} collective-permute-done((f32[2,16,576]{2,1,0:T(8,128)S(1)}, f32[2,16,576]{2,1,0:T(8,128)S(1)}, u32[]{:S(2)}, u32[]{:S(2)}) %collective-permute-start.4) | collective-permute-done | bytes 73760 | tf_op jit(solution)/shard_map/ppermute | solution.py:14
  129.2 0.6 slice.49
  129.8 4.5 %collective-permute-start.5 = (f32[1,16,576]{2,1,0:T(8,128)}, f32[1,16,576]{2,1,0:T(8,128)}, u32[]{:S(2)}, u32[]{:S(2)}) collective-permute-start(f32[1,16,576]{2,1,0:T(8,128)} %slice.49), channel_id=1, source_target_pairs={{8,0},{16,8},{24,16},{32,24},{40,32},{48,40},{56,48},{64,56},{72,6... | collective-permute-start | bytes 110600 | tf_op jit(solution)/shard_map/ppermute | solution.py:14
  134.3 0.5 fusion.8
  134.8 1.5 %copy.80 = bf16[128,8,512]{2,1,0:T(8,128)(2,1)} copy(bf16[128,8,512]{2,0,1:T(8,128)(2,1)S(1)} %multiply_convert_fusion) | data formatting | bytes 2097152
  136.4 0.8 copy.81
  137.2 2.0 %collective-permute-done.5 = f32[1,16,576]{2,1,0:T(8,128)} collective-permute-done((f32[1,16,576]{2,1,0:T(8,128)}, f32[1,16,576]{2,1,0:T(8,128)}, u32[]{:S(2)}, u32[]{:S(2)}) %collective-permute-start.5) | collective-permute-done | bytes 36896 | tf_op jit(solution)/shard_map/ppermute | solution.py:14
  139.1 0.8 fusion.19
  139.9 0.6 slice.51
  140.5 0.6 slice.50
  (32 shorter events, 0.2 us)
Async XLA Ops:
  0.6 23.8 %copy-start.2 = (bf16[128,8,512]{2,1,0:T(8,128)(2,1)S(1)}, bf16[128,8,512]{2,1,0:T(8,128)(2,1)}, u32[]{:S(2)}) copy-start(bf16[128,8,512]{2,1,0:T(8,128)(2,1)} %param.11) | copy-start | bytes 3145732
  2.5 6.2 %collective-permute-start = (bf16[1,128,576]{1,2,0:T(8,128)(2,1)S(1)}, bf16[1,128,576]{1,2,0:T(8,128)(2,1)S(1)}, u32[]{:S(2)}, u32[]{:S(2)}) collective-permute-start(bf16[1,128,576]{1,2,0:T(8,128)(2,1)S(1)} %maximum_bitcast_fusion), channel_id=1, source_target_pairs={{0,8},{8,16},{16,24},{24,32},{32,40},{40,48},{48,56},{56,64},{64,7... | collective-permute-start | bytes 442376 | tf_op jit(solution)/shard_map/ppermute | solution.py:14
  8.7 17.3 %copy-start.3 = (bf16[1,128,576]{1,2,0:T(8,128)(2,1)}, bf16[1,128,576]{1,2,0:T(8,128)(2,1)S(1)}, u32[]{:S(2)}) copy-start(bf16[1,128,576]{1,2,0:T(8,128)(2,1)S(1)} %collective-permute-done) | copy-start | bytes 442372
  8.7 11.4 %collective-permute-start.1 = (bf16[2,128,576]{1,2,0:T(8,128)(2,1)S(1)}, bf16[2,128,576]{1,2,0:T(8,128)(2,1)S(1)}, u32[]{:S(2)}, u32[]{:S(2)}) collective-permute-start(bf16[2,128,576]{1,2,0:T(8,128)(2,1)S(1)} %pad_maximum_fusion.3), channel_id=1, source_target_pairs={{0,16},{8,24},{16,32},{24,40},{32,48},{40,56},{48,64},{56,72},{64,... | collective-permute-start | bytes 884744 | tf_op jit(solution)/shard_map/ppermute | solution.py:14
  13.5 12.6 %copy-start.8 = (bf16[128,512]{1,0:T(8,128)(2,1)S(1)}, bf16[128,512]{1,0:T(8,128)(2,1)}, u32[]{:S(2)}) copy-start(bf16[128,512]{1,0:T(8,128)(2,1)} %param.9) | copy-start | bytes 393220
  15.5 25.5 %copy-start.1 = (bf16[128,8,512]{0,2,1:T(8,128)(2,1)}, bf16[128,8,512]{0,2,1:T(8,128)(2,1)S(1)}, u32[]{:S(2)}) copy-start(bf16[128,8,512]{0,2,1:T(8,128)(2,1)S(1)} %copy.70) | copy-start | bytes 3145732
  15.5 14.0 %copy-start.10 = (s32[128]{0:T(128)S(1)}, s32[128]{0:T(128)}, u32[]{:S(2)}) copy-start(s32[128]{0:T(128)} %param.15) | copy-start | bytes 1540
  20.1 9.4 %copy-start.4 = (bf16[2,128,576]{1,2,0:T(8,128)(2,1)}, bf16[2,128,576]{1,2,0:T(8,128)(2,1)S(1)}, u32[]{:S(2)}) copy-start(bf16[2,128,576]{1,2,0:T(8,128)(2,1)S(1)} %collective-permute-done.1) | copy-start | bytes 884740
  20.2 15.2 %collective-permute-start.2 = (bf16[4,128,576]{1,2,0:T(8,128)(2,1)S(1)}, bf16[4,128,576]{1,2,0:T(8,128)(2,1)}, u32[]{:S(2)}, u32[]{:S(2)}) collective-permute-start(bf16[4,128,576]{1,2,0:T(8,128)(2,1)S(1)} %pad_maximum_fusion.2), channel_id=1, source_target_pairs={{0,32},{8,40},{16,48},{24,56},{32,64},{40,72},{48,80},{56,88},{64,... | collective-permute-start | bytes 1769480 | tf_op jit(solution)/shard_map/ppermute | solution.py:14
  37.5 1.7 %copy-start.6 = (bf16[128,8,512]{0,2,1:T(8,128)(2,1)S(1)}, bf16[128,8,512]{0,2,1:T(8,128)(2,1)}, u32[]{:S(2)}) copy-start(bf16[128,8,512]{0,2,1:T(8,128)(2,1)} %copy.68) | copy-start | bytes 3145732
  37.5 1.7 %copy-start.9 = (pred[128,1024]{0,1:T(8,128)(4,1)S(1)}, pred[128,1024]{0,1:T(8,128)(4,1)}, u32[]{:S(2)}) copy-start(pred[128,1024]{0,1:T(8,128)(4,1)} %compare_and_fusion) | copy-start | bytes 393220
  37.6 1.7 %copy-start.11 = (f32[128,8]{0,1:T(8,128)S(1)}, f32[128,8]{0,1:T(8,128)}, u32[]{:S(2)}) copy-start(f32[128,8]{0,1:T(8,128)} %param.12) | copy-start | bytes 12292
  42.3 2.6 %copy-start.5 = (bf16[128,512]{0,1:T(8,128)(2,1)S(1)}, bf16[128,512]{0,1:T(8,128)(2,1)}, u32[]{:S(2)}) copy-start(bf16[128,512]{0,1:T(8,128)(2,1)} %copy.61) | copy-start | bytes 393220
  51.8 4.2 %copy-start = (f32[1024,576]{1,0:T(8,128)S(1)}, f32[1024,576]{1,0:T(8,128)}, u32[]{:S(2)}) copy-start(f32[1024,576]{1,0:T(8,128)} %copy.72) | copy-start | bytes 7077892
  92.3 24.9 %collective-permute-start.3 = (f32[4,16,576]{2,1,0:T(8,128)S(1)}, f32[4,16,576]{2,1,0:T(8,128)S(1)}, u32[]{:S(2)}, u32[]{:S(2)}) collective-permute-start(f32[4,16,576]{2,1,0:T(8,128)S(1)} %slice.45), channel_id=1, source_target_pairs={{32,0},{40,8},{48,16},{56,24},{64,32},{72,40},{80,48},{88,56},{96,... | collective-permute-start | bytes 442376 | tf_op jit(solution)/shard_map/ppermute | solution.py:14
  118.2 11.0 %collective-permute-start.4 = (f32[2,16,576]{2,1,0:T(8,128)S(1)}, f32[2,16,576]{2,1,0:T(8,128)S(1)}, u32[]{:S(2)}, u32[]{:S(2)}) collective-permute-start(f32[2,16,576]{2,1,0:T(8,128)S(1)} %slice.47), channel_id=1, source_target_pairs={{16,0},{24,8},{32,16},{40,24},{48,32},{56,40},{64,48},{72,56},{80,... | collective-permute-start | bytes 221192 | tf_op jit(solution)/shard_map/ppermute | solution.py:14
  129.2 0.7 copy-start.7
  129.8 9.3 %collective-permute-start.5 = (f32[1,16,576]{2,1,0:T(8,128)}, f32[1,16,576]{2,1,0:T(8,128)}, u32[]{:S(2)}, u32[]{:S(2)}) collective-permute-start(f32[1,16,576]{2,1,0:T(8,128)} %slice.49), channel_id=1, source_target_pairs={{8,0},{16,8},{24,16},{32,24},{40,32},{48,40},{56,48},{64,56},{72,6... | collective-permute-start | bytes 110600 | tf_op jit(solution)/shard_map/ppermute | solution.py:14
